TPU v7x, 32 devices: a whole 2x2x4 slice. The times are simulated.
32 devices in a mesh: groups: 2 (over y), seq: 4 (over z), head: 2 (over x), sub: 2 (over core).
Axes of the slice: x: 2, y: 2, z: 4, core: 2. Of those that a mesh axis runs over, the one named last changes fastest.
Arguments:
- queries: bfloat16 [64, 1024, 128], P(('head', 'sub'), ('groups', 'seq')), parts along dimension 1, may hold values from -6 to 6
- keys_values: bfloat16 [8, 1024, 256], P(('head', 'sub'), ('groups', 'seq')), parts along dimension 1, may hold values from -6 to 6
- student_x: bfloat16 [64, 1024, 128], P(('head', 'sub'), ('groups', 'seq')), parts along dimension 1, may hold values from -32 to 32
- state_maps: bfloat16 [8, 1024, 128], P(('head', 'sub'), ('groups', 'seq')), parts along dimension 1, may hold values from -0.75 to 0.75
- decay_logit: float32 [64, 1024], P(('head', 'sub'), ('groups', 'seq')), parts along dimension 1, may hold values from 0 to 16
- skip_gain: float32 [64], P(('head', 'sub')), may hold values from 0.5 to 2
- init_state: float32 [128, 64, 128], P(('groups', 'head', 'sub')), parts along dimension 0, may hold values from -6 to 6
Outputs:
- grad_x: bfloat16 [64, 1024, 128], P(('head', 'sub'), ('groups', 'seq')), parts along dimension 1
- grad_maps: bfloat16 [8, 1024, 128], P(('head', 'sub'), ('groups', 'seq')), parts along dimension 1
- grad_log_decay: float32 [64, 1024], P(('head', 'sub'), ('groups', 'seq')), parts along dimension 1
There are 2 independent parts, one for each index of `groups`. A program takes and returns all parts, laid end to end along the dimension named above; an argument that names none is the same for every part. Nothing has to cross between parts.
All inputs are finite; a program needn't handle non-finite values.
Results may differ from a plain program's by a relative error of at most 0.013.
Values may be sent and summed in bfloat16 or wider, within the bound.
No kernel may reach another device: no remote copies, remote signals or barrier semaphores. Data moves between devices by JAX's collectives and lax.ppermute only.
A program may use at most 64 MiB of HBM per device.

v0:
```python
import math
import jax
import jax.numpy as jnp
from jax import lax
from jax.sharding import PartitionSpec as P

epsilon = 1e-05
highest = lax.Precision.HIGHEST


def entering_2(x, axis, join, neutral):
    place = lax.axis_index(axis)
    gathered = jax.tree.map(
        lambda a, kind: lax.all_gather(a.astype(kind), axis), x, (jnp.bfloat16, jnp.bfloat16)
    )
    state = jax.tree.map(lambda a, e: jnp.zeros_like(a) + jnp.asarray(e, a.dtype), x, neutral)

    def entering_one(turn, state):
        return join(
            state,
            jax.tree.map(
                lambda a, own: lax.dynamic_index_in_dim(a, turn, 0, False).astype(own.dtype),
                gathered,
                x,
            ),
        )

    return lax.fori_loop(0, place, entering_one, state)


def prefix(x, axis, join, neutral):
    count = lax.axis_size(axis)
    place = lax.axis_index(axis)
    ahead = count - 1 - place
    gathered = jax.tree.map(
        lambda a, kind: lax.all_gather(a.astype(kind), axis),
        x,
        jax.tree.map(lambda a: jnp.bfloat16 if a.dtype == jnp.float32 else a.dtype, x),
    )
    state = jax.tree.map(lambda a, e: jnp.zeros_like(a) + jnp.asarray(e, a.dtype), x, neutral)

    def prefix_one(turn, state):
        source = count - 1 - turn
        return join(
            state,
            jax.tree.map(
                lambda a, own: lax.dynamic_index_in_dim(a, source, 0, False).astype(own.dtype),
                gathered,
                x,
            ),
        )

    return lax.fori_loop(0, ahead, prefix_one, state)


def attend(query_rows, positions, keys_values, tok_dev):
    group_count, row_count, head_width = query_rows.shape
    score_scale = head_width ** (-0.5)
    start_max = jnp.full((group_count, row_count), -1e30, jnp.float32)
    start_sum = jnp.zeros((group_count, row_count), jnp.float32)
    start_acc = jnp.zeros((group_count, row_count, head_width), jnp.float32)
    shards = lax.all_gather(keys_values, "seq", axis=1, tiled=True)
    block_rows = math.gcd(shards.shape[1], tok_dev)

    def one_block(number, running):
        running_max, running_sum, weighted = running
        key_block = lax.dynamic_slice_in_dim(shards, number * block_rows, block_rows, 1)
        scores = (
            jnp.einsum(
                "grd,gkd->grk",
                query_rows,
                key_block[:, :, :head_width],
                preferred_element_type=jnp.float32,
            )
            * score_scale
        )
        key_positions = number * block_rows + jnp.arange(block_rows)
        allowed = (positions[:, None] >= key_positions[None, :])[None]
        scores = jnp.where(allowed, scores, -1e30)
        new_max = jnp.maximum(running_max, jnp.max(scores, axis=2))
        weights = jnp.where(allowed, jnp.exp(scores - new_max[..., None]), 0.0)
        factor = jnp.exp(running_max - new_max)
        running_sum = running_sum * factor + jnp.sum(weights, axis=2)
        weighted = weighted * factor[..., None] + jnp.einsum(
            "grk,gkd->grd",
            weights.astype(jnp.bfloat16),
            key_block[:, :, head_width:],
            preferred_element_type=jnp.float32,
        )
        return (new_max, running_sum, weighted)

    running_max, running_sum, weighted = lax.fori_loop(
        0, shards.shape[1] // block_rows, one_block, (start_max, start_sum, start_acc)
    )
    return (weighted / running_sum[..., None]).astype(jnp.bfloat16)


def forward_chain(earlier, later):
    return (earlier[0] * later[0], later[0][:, None, None] * earlier[1] + later[1])


def backward_chain(earlier, later):
    decay_early, state_early, closing_early, sums_early = earlier
    decay_late, state_late, closing_late, sums_late = later
    return (
        decay_early * decay_late,
        decay_late[:, None, None] * state_early + state_late,
        closing_early + decay_early[:, None, None] * closing_late,
        sums_early + sums_late - jnp.sum(closing_late * state_early, axis=(1, 2)),
    )


def body(queries, keys_values, student_x, state_maps, decay_logit, skip_gain, init_state):
    local_heads, tok_dev, head_width = student_x.shape
    local_groups = state_maps.shape[0]
    per_group = local_heads // local_groups
    state_size = state_maps.shape[2] // 2
    seq_count = lax.axis_size("seq")
    seq_rank = lax.axis_index("seq")
    repeat_count = max(1, seq_count // per_group)
    sub_rows = tok_dev // repeat_count
    per_peer = per_group * repeat_count // seq_count
    sectioned = queries.reshape(local_groups, per_group * repeat_count, sub_rows, head_width)
    arrived = lax.all_to_all(sectioned, "seq", split_axis=1, concat_axis=1, tiled=True)
    slot_ids = jnp.arange(seq_count * per_peer)
    source = slot_ids // per_peer
    member = seq_rank * per_peer + slot_ids % per_peer
    starts = source * tok_dev + member % repeat_count * sub_rows
    positions = (starts[:, None] + jnp.arange(sub_rows)[None, :]).reshape(-1)
    answers = attend(arrived.reshape(local_groups, -1, head_width), positions, keys_values, tok_dev)
    answers = answers.reshape(local_groups, seq_count * per_peer, sub_rows, head_width)
    teacher = lax.all_to_all(answers, "seq", split_axis=1, concat_axis=1, tiled=True).reshape(
        local_heads, tok_dev, head_width
    )
    teacher_wide = teacher.astype(jnp.float32)
    target = teacher_wide * lax.rsqrt(
        jnp.mean(teacher_wide * teacher_wide, axis=2, keepdims=True) + epsilon
    )
    log_decay = jax.nn.log_sigmoid(decay_logit)
    cumulative = jnp.cumsum(log_decay, axis=1)
    totals = cumulative[:, -1]
    decays = jnp.exp(totals)
    to_end = jnp.exp(totals[:, None] - cumulative)
    from_start = jnp.exp(cumulative)
    in_maps = state_maps[:, :, :state_size]
    out_maps = state_maps[:, :, state_size:]
    intersection = jnp.einsum("gtn,gsn->gts", out_maps, in_maps, preferred_element_type=jnp.float32)
    order_ids = jnp.arange(tok_dev)
    causal = (order_ids[:, None] >= order_ids[None, :])[None]
    gaps = cumulative[:, :, None] - cumulative[:, None, :]
    decayed = jnp.where(causal, jnp.exp(jnp.where(causal, gaps, 0.0)), 0.0)
    mixing = (
        decayed.reshape(local_groups, per_group, tok_dev, tok_dev) * intersection[:, None]
    ).reshape(local_heads, tok_dev, tok_dev)
    inputs_wide = student_x.astype(jnp.float32)
    in_heads = jnp.repeat(in_maps.astype(jnp.float32), per_group, axis=0)
    out_heads = jnp.repeat(out_maps.astype(jnp.float32), per_group, axis=0)
    local_out = jnp.einsum("hts,hsp->htp", mixing, inputs_wide, precision=highest)
    weighted_in = in_heads * to_end[..., None]
    end_state = jnp.einsum("hsn,hsp->hnp", weighted_in, inputs_wide, precision=highest)
    prefix_decay, prefix_state = entering_2(
        (decays, end_state),
        "seq",
        forward_chain,
        (jnp.ones_like(decays), jnp.zeros_like(end_state)),
    )
    entering = prefix_state + prefix_decay[:, None, None] * init_state
    state_out = local_out + from_start[..., None] * jnp.einsum(
        "htn,hnp->htp", out_heads, entering, precision=highest
    )
    outputs = state_out + skip_gain[:, None, None] * inputs_wide
    inverse = lax.rsqrt(jnp.mean(outputs * outputs, axis=2, keepdims=True) + epsilon)
    normed = outputs * inverse
    residual = normed - target
    grad_out = (residual - normed * jnp.mean(residual * normed, axis=2, keepdims=True)) * inverse
    local_dx = jnp.einsum("hts,htp->hsp", mixing, grad_out, precision=highest)
    cross = jnp.einsum("htp,hsp->hts", grad_out, inputs_wide, precision=highest)
    paired = decayed * cross
    local_din = jnp.einsum("hts,htn->hsn", paired, out_heads, precision=highest)
    grad_output_maps = jnp.einsum("hts,hsn->htn", paired, in_heads, precision=highest)
    grad_output_maps = grad_output_maps + from_start[..., None] * jnp.einsum(
        "hnp,htp->htn", entering, grad_out, precision=highest
    )
    forward_term = jnp.sum(grad_out * state_out, axis=2)
    flow = jnp.einsum(
        "htn,htp->hnp", out_heads * from_start[..., None], grad_out, precision=highest
    )
    closing = jnp.sum(forward_term - jnp.sum(inputs_wide * local_dx, axis=2), axis=1)
    identity = (
        jnp.ones_like(decays),
        jnp.zeros_like(flow),
        jnp.zeros_like(end_state),
        jnp.zeros_like(closing),
    )
    unused_decay, incoming, unused_state, later_sum = prefix(
        (decays, flow, end_state, closing), "seq", backward_chain, identity
    )
    state_dx = local_dx + jnp.einsum("hsn,hnp->hsp", weighted_in, incoming, precision=highest)
    terms = forward_term - jnp.sum(inputs_wide * state_dx, axis=2)
    grad_log_decay = later_sum[:, None] + lax.cumsum(terms, axis=1, reverse=True)
    grad_input_maps = (
        local_din
        + jnp.einsum("hnp,hsp->hsn", incoming, inputs_wide, precision=highest) * to_end[..., None]
    )
    grad_maps = jnp.concatenate([grad_input_maps, grad_output_maps], axis=2)
    grad_maps = grad_maps.reshape(local_groups, per_group, tok_dev, 2 * state_size).sum(axis=1)
    grad_x = state_dx + skip_gain[:, None, None] * grad_out
    return (grad_x.astype(jnp.bfloat16), grad_maps.astype(jnp.bfloat16), grad_log_decay)


def solution(mesh):
    in_specs = (
        P(("head", "sub"), ("groups", "seq"), None),
        P(("head", "sub"), ("groups", "seq"), None),
        P(("head", "sub"), ("groups", "seq"), None),
        P(("head", "sub"), ("groups", "seq"), None),
        P(("head", "sub"), ("groups", "seq")),
        P(("head", "sub")),
        P(("groups", "head", "sub"), None, None),
    )
    out_specs = (
        P(("head", "sub"), ("groups", "seq"), None),
        P(("head", "sub"), ("groups", "seq"), None),
        P(("head", "sub"), ("groups", "seq")),
    )
    return jax.shard_map(body, mesh=mesh, in_specs=in_specs, out_specs=out_specs, check_vma=False)
```

profile of v0, /device:TPU:0, one launch (start us, length us, event | category | flops | bytes accessed | tf_op | source)
XLA Modules:
  0.0 146.4 jit_solution(11512429082375482874)
XLA Ops:
  8.9 1.2 convolution_convert_fusion.1
  10.9 6.3 %all-to-all-start = ((bf16[2,8,128,128]{3,2,0,1:T(8,128)(2,1)}), bf16[2,8,128,128]{3,2,0,1:T(8,128)(2,1)S(1)}, u32[]{:S(2)}, u32[]{:S(2)}) async-start(bf16[2,8,128,128]{3,2,0,1:T(8,128)(2,1)} %copy.89), calls=%async_computation | async-start | bytes 1048576 | tf_op jit(solution)/shard_map/all_to_all | solution.py:124
  19.9 18.1 %all-reduce = bf16[64]{0:T(256)(128)(2,1)S(1)} all-reduce(bf16[64]{0:T(256)(128)(2,1)S(1)} %dynamic-update-slice), channel_id=2, replica_groups=mesh['groups'=2,'seq'=4,'head'=2,'sub'=2] {'seq'}, use_global_device_ids=true, to_apply=%add | all-reduce | flops 64 | bytes 256
  39.3 23.4 %all_gather.30 = bf16[2,512,256]{2,1,0:T(8,128)(2,1)} all-gather(bf16[2,128,256]{2,1,0:T(8,128)(2,1)S(1)} %copy-done.17), channel_id=1, replica_groups=mesh['groups'=2,'seq'=4,'head'=2,'sub'=2] {'seq'}, dimensions={1}, use_global_device_ids=true | all-gather | bytes 655360 | tf_op jit(solution)/shard_map/all_gather | solution.py:62
  62.8 2.2 %fusion.49 = f32[16,128,128]{1,2,0:T(8,128)} fusion(f32[16,128,128]{2,1,0:T(8,128)S(1)} %bitcast_multiply_fusion.1, bf16[16,128,128]{2,1,0:T(8,128)(2,1)S(1)} %copy-done), kind=kOutput, calls=%fused_computation.102 | convolution fusion | flops 402653184 | bytes 2621440 | tf_op jit(solution)/shard_map/hts,hsp->htp/dot_general | solution.py:158
  65.0 13.6 %while.49 = (s32[]{:T(128)}, f32[2,1024]{1,0:T(2,128)S(1)}, f32[2,1024]{1,0:T(2,128)S(1)}, f32[2,1024,128]{2,1,0:T(8,128)S(1)}, bf16[2,512,256]{2,1,0:T(8,128)(2...) while((s32[]{:T(128)}, f32[2,1024]{1,0:T(2,128)S(1)}, ...), condition=%wide.region_7.8_spmd.clone, body=%wide.region_4.7_spmd.clone.sunk | while | flops 137505920 | bytes 6563051 | solution.py:92
  65.3 1.2 fusion.86
  66.8 1.6 %convolution_add_fusion.5 = f32[2,1024,128]{2,1,0:T(8,128)S(1)} fusion(f32[2,1024,128]{2,1,0:T(8,128)S(1)} %get-tuple-element.598, f32[2,1024,128]{1,2,0:T(8,128)S(1)} %get-tuple-element.553, f32[2,1024]{1,0:T(2,128)S(1)} %get-tuple-element.555, f32[2,1024]{1,0:T(2,128)S(1)} %fusion.87, pred[]{:T(512)S(6)} %compare.10, ...), kind=kOutput, calls=%fused_computation.14.clone.1 | convolution fusion | flops 68681728 | bytes 3358729 | tf_op jit(solution)/shard_map/while/body/eval_jaxpr/grk,gkd->grd/dot_general | solution.py:84
  68.7 1.2 fusion.86
  70.2 1.6 %convolution_add_fusion.5 = f32[2,1024,128]{2,1,0:T(8,128)S(1)} fusion(f32[2,1024,128]{2,1,0:T(8,128)S(1)} %get-tuple-element.598, f32[2,1024,128]{1,2,0:T(8,128)S(1)} %get-tuple-element.553, f32[2,1024]{1,0:T(2,128)S(1)} %get-tuple-element.555, f32[2,1024]{1,0:T(2,128)S(1)} %fusion.87, pred[]{:T(512)S(6)} %compare.10, ...), kind=kOutput, calls=%fused_computation.14.clone.1 | convolution fusion | flops 68681728 | bytes 3358729 | tf_op jit(solution)/shard_map/while/body/eval_jaxpr/grk,gkd->grd/dot_general | solution.py:84
  72.1 1.2 fusion.86
  73.6 1.6 %convolution_add_fusion.5 = f32[2,1024,128]{2,1,0:T(8,128)S(1)} fusion(f32[2,1024,128]{2,1,0:T(8,128)S(1)} %get-tuple-element.598, f32[2,1024,128]{1,2,0:T(8,128)S(1)} %get-tuple-element.553, f32[2,1024]{1,0:T(2,128)S(1)} %get-tuple-element.555, f32[2,1024]{1,0:T(2,128)S(1)} %fusion.87, pred[]{:T(512)S(6)} %compare.10, ...), kind=kOutput, calls=%fused_computation.14.clone.1 | convolution fusion | flops 68681728 | bytes 3358729 | tf_op jit(solution)/shard_map/while/body/eval_jaxpr/grk,gkd->grd/dot_general | solution.py:84
  75.5 1.2 fusion.86
  77.0 1.6 %convolution_add_fusion.5 = f32[2,1024,128]{2,1,0:T(8,128)S(1)} fusion(f32[2,1024,128]{2,1,0:T(8,128)S(1)} %get-tuple-element.598, f32[2,1024,128]{1,2,0:T(8,128)S(1)} %get-tuple-element.553, f32[2,1024]{1,0:T(2,128)S(1)} %get-tuple-element.555, f32[2,1024]{1,0:T(2,128)S(1)} %fusion.87, pred[]{:T(512)S(6)} %compare.10, ...), kind=kOutput, calls=%fused_computation.14.clone.1 | convolution fusion | flops 68681728 | bytes 3358729 | tf_op jit(solution)/shard_map/while/body/eval_jaxpr/grk,gkd->grd/dot_general | solution.py:84
  80.0 3.5 %all-to-all-start.1 = ((bf16[2,8,128,128]{2,3,0,1:T(8,128)(2,1)}), bf16[2,8,128,128]{2,3,0,1:T(8,128)(2,1)S(1)}, u32[]{:S(2)}, u32[]{:S(2)}) async-start(bf16[2,8,128,128]{2,3,0,1:T(8,128)(2,1)} %copy.91), calls=%async_computation.1 | async-start | bytes 1048576 | tf_op jit(solution)/shard_map/all_to_all | solution.py:132
  83.9 1.1 copy-done.14
  85.1 3.3 %multiply_reduce_fusion.3 = (f32[16,128]{1,0:T(8,128)S(1)}, f32[16,128,128]{1,2,0:T(8,128)S(1)}) fusion(bf16[16,128,128]{1,2,0:T(8,128)(2,1)S(1)} %copy.88, f32[16]{0:T(128)S(1)} %copy-done.18, f32[16,128,128]{1,2,0:T(8,128)} %fusion.49, f32[16,128,64]{1,2,0:T(8,128)S(1)} %bitcast.93, f32[16,64,128]{2,1,0:T(8,128)S(1)} %get-tuple-element.293, ...), kind=kOutput, calls=%fused_computation.67 | convolution fusion | flops 203421696 | bytes 4210816 | tf_op jit(solution)/shard_map/htn,hnp->htp/dot_general | solution.py:168
  88.4 5.4 %all-to-all-done.1 = bf16[2,8,128,128]{2,3,0,1:T(8,128)(2,1)S(1)} async-done(((bf16[2,8,128,128]{2,3,0,1:T(8,128)(2,1)}), bf16[2,8,128,128]{2,3,0,1:T(8,128)(2,1)S(1)}, u32[]{:S(2)}, u32[]{:S(2)}) %all-to-all-start.1) | async-done | bytes 524320 | tf_op jit(solution)/shard_map/all_to_all | solution.py:132
  95.5 2.8 %convolution_convert_fusion = bf16[16,64,128]{2,1,0:T(8,128)(2,1)} fusion(f32[16,128,128]{1,2,0:T(8,128)S(1)} %get-tuple-element.394, f32[16,128,64]{1,2,0:T(8,128)S(1)} %bitcast.94, f32[16,128]{1,0:T(8,128)S(1)} %get-tuple-element.404), kind=kOutput, calls=%fused_computation.51 | convolution fusion | flops 201588736 | bytes 1843200 | tf_op jit(solution)/shard_map/htn,htp->hnp/dot_general | solution.py:185
  98.3 2.2 %fusion.28 = (f32[16,128]{1,0:T(8,128)S(1)}, f32[16,128,128]{1,2,0:T(8,128)}) fusion(bf16[16,128,128]{1,2,0:T(8,128)(2,1)S(1)} %copy.88, f32[16,128,128]{2,1,0:T(8,128)S(1)} %copy-done.3, f32[16,128,128]{1,2,0:T(8,128)S(1)} %get-tuple-element.394), kind=kOutput, calls=%fused_computation.54 | convolution fusion | flops 403437568 | bytes 3678208 | tf_op jit(solution)/shard_map/hts,htp->hsp/dot_general | solution.py:176
  100.9 10.3 %all-reduce.1 = bf16[64]{0:T(256)(128)(2,1)S(1)} all-reduce(bf16[64]{0:T(256)(128)(2,1)S(1)} %dynamic-update-slice.1), channel_id=5, replica_groups=mesh['groups'=2,'seq'=4,'head'=2,'sub'=2] {'seq'}, use_global_device_ids=true, to_apply=%add.1 | all-reduce | flops 64 | bytes 256
  111.2 2.2 %convolution_multiply_fusion.3 = f32[16,128,64]{1,2,0:T(8,128)S(1)} fusion(f32[16,128,128]{1,2,0:T(8,128)S(1)} %get-tuple-element.394, f32[16,128]{1,0:T(8,128)S(1)} %get-tuple-element.404, f32[16,64,128]{2,1,0:T(8,128)S(1)} %get-tuple-element.293, f32[16,64,128]{2,1,0:T(8,128)} %param.19, f32[16]{0:T(128)S(1)} %get-tuple-element.294), kind=kOutput, calls=%fused_computation.46 | convolution fusion | flops 201719808 | bytes 2629696 | tf_op jit(solution)/shard_map/hnp,htp->htn/dot_general | solution.py:181
  113.4 1.2 convolution_multiply_fusion.1
  115.7 2.9 %convolution_add_fusion.2 = f32[16,128,64]{1,2,0:T(8,128)} fusion(f32[16,128,64]{1,2,0:T(8,128)S(1)} %convolution_multiply_fusion.3, f32[16,128,128]{2,1,0:T(8,128)S(1)} %convolution_multiply_fusion.1, f32[16,128,64]{1,2,0:T(8,128)S(1)} %bitcast.97), kind=kOutput, calls=%fused_computation.47 | convolution fusion | flops 201457664 | bytes 2621440 | tf_op jit(solution)/shard_map/hts,hsn->htn/dot_general | solution.py:180
  118.6 7.5 %all-gather.9.cloned.1.call-done = bf16[64,64,128]{2,1,0:T(8,128)(2,1)} async-done(((bf16[16,64,128]{2,1,0:T(8,128)(2,1)}), bf16[64,64,128]{2,1,0:T(8,128)(2,1)}) %all-gather.9.cloned.1.call-update) | async-done | bytes 1048592 | tf_op jit(solution)/shard_map/all_gather | solution.py:36
  126.1 4.4 %while.48 = (s32[]{:T(128)}, f32[16,64,128]{2,1,0:T(8,128)S(1)}, f32[16]{0:T(128)S(1)}, s32[]{:T(128)}, bf16[4,16]{1,0:T(4,128)(2,1)S(1)}, /*index=5*/bf16[4,16,...) while((s32[]{:T(128)}, f32[16,64,128]{2,1,0:T(8,128)S(1)}, ...), condition=%wide.region_15.16_spmd, body=%wide.region_13.15_spmd.sunk | while | flops 786486 | bytes 1573487 | solution.py:53
  126.2 1.3 fusion.81
  127.5 1.3 fusion.81
  128.9 1.3 fusion.81
  130.5 1.1 fusion.26
  131.7 2.8 %fusion.29 = (f32[16,128]{1,0:T(8,128)S(1)}, bf16[16,128,128]{1,2,0:T(8,128)(2,1)}) fusion(bf16[16,128,128]{1,2,0:T(8,128)(2,1)S(1)} %copy.88, f32[16,128,128]{1,2,0:T(8,128)S(1)} %get-tuple-element.394, f32[16]{0:T(128)S(1)} %copy-done.18, f32[16,128,128]{1,2,0:T(8,128)S(1)} %copy-done.11, f32[16,64,128]{2,1,0:T(8,128)S(1)} %get-tuple-element.297, ...), kind=kOutput, calls=%fused_computation.55 | convolution fusion | flops 203290624 | bytes 4210752 | tf_op jit(solution)/shard_map/hsn,hnp->hsp/dot_general | solution.py:198
  137.6 1.2 reduce_window_sum.22
  (127 shorter events, 16.5 us)
Async XLA Ops:
  7.2 1.4 copy-start.15
  7.2 1.7 %copy-start = (bf16[16,128,128]{2,1,0:T(8,128)(2,1)S(1)}, bf16[16,128,128]{2,1,0:T(8,128)(2,1)}, u32[]{:S(2)}) copy-start(bf16[16,128,128]{2,1,0:T(8,128)(2,1)} %param.15) | copy-start | bytes 1572868
  7.2 76.4 %all-gather.7.cloned.1.call-start = ((), (), s32[]{:S(2)}) async-start(), calls=%async_computation.2 | async-start | bytes 1310720 | tf_op jit(solution)/shard_map/all_gather | solution.py:14
  8.8 1.3 copy-start.9
  8.8 1.3 copy-start.16
  10.9 54.0 %all-to-all-start = ((bf16[2,8,128,128]{3,2,0,1:T(8,128)(2,1)}), bf16[2,8,128,128]{3,2,0,1:T(8,128)(2,1)S(1)}, u32[]{:S(2)}, u32[]{:S(2)}) async-start(bf16[2,8,128,128]{3,2,0,1:T(8,128)(2,1)} %copy.89), calls=%async_computation | async-start | bytes 1048576 | tf_op jit(solution)/shard_map/all_to_all | solution.py:124
  17.8 0.7 copy-start.19
  38.4 0.9 copy-start.17
  38.8 24.0 %copy-start.2 = (f32[16,128,128]{2,1,0:T(8,128)}, f32[16,128,128]{2,1,0:T(8,128)S(1)}, u32[]{:S(2)}) copy-start(f32[16,128,128]{2,1,0:T(8,128)S(1)} %bitcast_multiply_fusion.1) | copy-start | bytes 3145732
  80.0 13.7 %all-to-all-start.1 = ((bf16[2,8,128,128]{2,3,0,1:T(8,128)(2,1)}), bf16[2,8,128,128]{2,3,0,1:T(8,128)(2,1)S(1)}, u32[]{:S(2)}, u32[]{:S(2)}) async-start(bf16[2,8,128,128]{2,3,0,1:T(8,128)(2,1)} %copy.91), calls=%async_computation.1 | async-start | bytes 1048576 | tf_op jit(solution)/shard_map/all_to_all | solution.py:132
  83.5 42.5 %all-gather.9.cloned.1.call-start = ((), (), s32[]{:S(2)}) async-start(), calls=%async_computation.3 | async-start | bytes 1310720 | tf_op jit(solution)/shard_map/all_gather | solution.py:36
  83.8 1.2 copy-start.14
  83.9 4.4 %copy-start.6 = (f32[2,8,128,64]{2,3,1,0:T(8,128)}, f32[2,8,128,64]{2,3,1,0:T(8,128)S(1)}, u32[]{:S(2)}) copy-start(f32[2,8,128,64]{2,3,1,0:T(8,128)S(1)} %broadcast_in_dim.109) | copy-start | bytes 1572868
  83.9 1.2 copy-start.18
  94.4 1.0 copy-start.7
  95.5 2.9 %copy-start.3 = (f32[16,128,128]{2,1,0:T(8,128)S(1)}, f32[16,128,128]{2,1,0:T(8,128)}, u32[]{:S(2)}) copy-start(f32[16,128,128]{2,1,0:T(8,128)} %copy-done.2) | copy-start | bytes 3145732
  111.2 2.2 %copy-start.1 = (bf16[16,128,128]{2,1,0:T(8,128)(2,1)S(1)}, bf16[16,128,128]{2,1,0:T(8,128)(2,1)}, u32[]{:S(2)}) copy-start(bf16[16,128,128]{2,1,0:T(8,128)(2,1)} %param.15) | copy-start | bytes 1572868
  113.4 2.2 %copy-start.10 = (f32[2,8,128,64]{2,3,1,0:T(8,128)S(1)}, f32[2,8,128,64]{2,3,1,0:T(8,128)}, u32[]{:S(2)}) copy-start(f32[2,8,128,64]{2,3,1,0:T(8,128)} %copy-done.9) | copy-start | bytes 1572868
  114.7 1.0 copy-start.4
  130.5 1.2 copy-start.11
  131.7 2.8 %copy-start.5 = (f32[16,128,128]{2,1,0:T(8,128)S(1)}, f32[16,128,128]{2,1,0:T(8,128)}, u32[]{:S(2)}) copy-start(f32[16,128,128]{2,1,0:T(8,128)} %copy-done.4) | copy-start | bytes 3145732
  131.7 2.8 %copy-start.8 = (f32[2,8,128,64]{2,3,1,0:T(8,128)S(1)}, f32[2,8,128,64]{2,3,1,0:T(8,128)}, u32[]{:S(2)}) copy-start(f32[2,8,128,64]{2,3,1,0:T(8,128)} %copy-done.6) | copy-start | bytes 1572868
  134.5 1.1 copy-start.12
  135.6 1.0 copy-start.13
Sparse Core Ops, SparseCore 0:
  10.2 41.8 all-gather.6
  98.5 27.5 all-gather.8
where the time goes:
time: 147 us; the launch traced here: 146 us
  blocking collectives  51.8 us (35%)
  matrix products  34.5 us (23%)
  between operations  15.2 us (10%)
  waiting for transfers between devices  12.9 us (9%)
  other arithmetic  11.2 us (8%)
  local copies, waits for them, and re-layouts  10.1 us (7%)
  starting transfers between devices  9.87 us (7%)
    unnamed x2, blocking collectives  28.3 us
    all_gather x1, blocking collectives, attend(): shards = lax.all_gather(keys_values, 'seq', axis=1, tiled=True)  23.4 us
    unnamed x51, local copies, waits for them, and re-layouts  7.57 us
    all_gather x1, waiting for transfers between devices, prefix(): lax.all_gather(a.astype(kind), axis)  7.49 us
    dot_general x4, matrix products, one_block(): jnp.einsum('grk,gkd->grd', weights.astype(jnp.bfloat16), key_block[:, :,...  6.51 us
    all_to_all x1, starting transfers between devices, body(): lax.all_to_all(sectioned, 'seq', split_axis=1, concat_axis=1, tiled=True)  6.32 us
    all_to_all x1, waiting for transfers between devices, body(): lax.all_to_all(answers, 'seq', split_axis=1, concat_axis=1, tiled=True)  5.39 us
    dot_general x4, matrix products, one_block(): jnp.einsum('grd,gkd->grk', query_rows, key_block[:, :, :head_width], pref...  4.86 us
  transfers between devices with their start and end apart: 4, of which 2 were waited for; matrix products, arithmetic and copies ran while one was open for 22% of the time, Pallas kernels for 0%

commit v1 on v0

--- a/solution.py
+++ b/solution.py
@@ -1,3 +1,4 @@
+import functools
 import math
 import jax
 import jax.numpy as jnp
@@ -6,6 +7,41 @@
 
 epsilon = 1e-05
 highest = lax.Precision.HIGHEST
+
+
+def entries_close(values, array_dim, vec):
+    g_now = values.shape
+    big = values.reshape(*g_now[:array_dim], vec, g_now[array_dim] // vec, *g_now[array_dim + 1 :])
+    res = jnp.moveaxis(big, array_dim, 0)
+    return res
+
+
+def close_panel(sample, d_out):
+    f_next = list(sample.shape[1:])
+    f_next[d_out] *= sample.shape[0]
+    moved = jnp.moveaxis(sample, 0, d_out).reshape(f_next)
+    return moved
+
+
+def _convert_surface(page, comm_axis, x0, local_array):
+    x_new, z1 = (jax.lax.axis_size(comm_axis), jax.lax.axis_index(comm_axis))
+    o_now = entries_close(page, x0, x_new)
+    pieces_in = [o_now[z1]]
+    d = 1
+    while d < x_new:
+        f_now = o_now[(z1 + d) % x_new]
+        pieces_in.append(
+            jax.lax.ppermute(
+                f_now, axis_name=comm_axis, perm=[(q, (q + d) % x_new) for q in range(x_new)]
+            )
+        )
+        d = d + 1
+    o_now = jnp.stack(pieces_in)[(z1 - jnp.arange(x_new)) % x_new]
+    item_now = close_panel(o_now, local_array)
+    return item_now
+
+
+note_the_windows = functools.partial(_convert_surface, comm_axis="seq", x0=1, local_array=1)
 
 
 def entering_2(x, axis, join, neutral):
@@ -121,7 +157,7 @@
     sub_rows = tok_dev // repeat_count
     per_peer = per_group * repeat_count // seq_count
     sectioned = queries.reshape(local_groups, per_group * repeat_count, sub_rows, head_width)
-    arrived = lax.all_to_all(sectioned, "seq", split_axis=1, concat_axis=1, tiled=True)
+    arrived = note_the_windows(sectioned)
     slot_ids = jnp.arange(seq_count * per_peer)
     source = slot_ids // per_peer
     member = seq_rank * per_peer + slot_ids % per_peer

time: 147 us -> 143 us (0.973)
  waiting for transfers between devices: 12.9 us -> 6.24 us
  blocking collectives: 51.8 us -> 48.2 us
  local copies, waits for them, and re-layouts: 10.1 us -> 12.7 us
    ppermute x0 -> x3, starting transfers between devices: none -> 7.01 us  [_convert_surface(): jax.lax.ppermute(f_now, axis_name=comm_axis, perm=[(q, (q + d) % x_new) f...]
    all_to_all x1 -> x0, starting transfers between devices: 6.32 us -> none  [body(): lax.all_to_all(sectioned, 'seq', split_axis=1, concat_axis=1, tiled=True)]
    all_to_all x1, waiting for transfers between devices: 5.39 us -> 0.01 us  [body(): lax.all_to_all(answers, 'seq', split_axis=1, concat_axis=1, tiled=True)]
    unnamed x2, blocking collectives: 28.3 us -> 24.5 us
    unnamed x51 -> x45, local copies, waits for them, and re-layouts: 7.57 us -> 9.21 us
  transfers between devices with their start and end apart: 4 -> 6, of which waited for: 2 -> 1; matrix products, arithmetic and copies ran while one was open for 22% -> 23% of each run, Pallas kernels for 0% -> 0%
where the time goes in v1:
time: 143 us; the launch traced here: 142 us
  blocking collectives  48.2 us (34%)
  matrix products  35.7 us (25%)
  between operations  15.1 us (11%)
  local copies, waits for them, and re-layouts  12.7 us (9%)
  other arithmetic  11.8 us (8%)
  starting transfers between devices  11.3 us (8%)
  waiting for transfers between devices  6.24 us (4%)
    unnamed x2, blocking collectives  24.5 us
    all_gather x1, blocking collectives, attend(): shards = lax.all_gather(keys_values, 'seq', axis=1, tiled=True)  23.7 us
    unnamed x45, local copies, waits for them, and re-layouts  9.21 us
    ppermute x3, starting transfers between devices, _convert_surface(): jax.lax.ppermute(f_now, axis_name=comm_axis, perm=[(q, (q + d) % x_new) f...  7.01 us
    dot_general x4, matrix products, one_block(): jnp.einsum('grk,gkd->grd', weights.astype(jnp.bfloat16), key_block[:, :,...  6.51 us
    all_gather x1, waiting for transfers between devices, prefix(): lax.all_gather(a.astype(kind), axis)  6.18 us
    dot_general x4, matrix products, one_block(): jnp.einsum('grd,gkd->grk', query_rows, key_block[:, :, :head_width], pref...  4.86 us
    all_to_all x1, starting transfers between devices, body(): lax.all_to_all(answers, 'seq', split_axis=1, concat_axis=1, tiled=True)  4.27 us
  transfers between devices with their start and end apart: 6, of which 1 were waited for; matrix products, arithmetic and copies ran while one was open for 23% of the time, Pallas kernels for 0%

profile of v1, /device:TPU:0, one launch (start us, length us, event | category | flops | bytes accessed | tf_op | source)
XLA Modules:
  0.0 142.0 jit_solution(13874631146100308465)
XLA Ops:
  8.5 3.1 %collective-permute-start = (bf16[2,2,128,128]{3,2,1,0:T(8,128)(2,1)S(1)}, bf16[2,2,128,128]{3,2,1,0:T(8,128)(2,1)S(1)}, u32[]{:S(2)}, u32[]{:S(2)}) collective-permute-start(bf16[2,2,128,128]{3,2,1,0:T(8,128)(2,1)S(1)} %get-tuple-element.406), channel_id=1, source_target_pairs={{0,4},{4,8},{8,12},{12,0},{1,5},{5,9},{9,13},{13,1},{2,6},{6,10},{... | collective-permute-start | bytes 393224 | tf_op jit(solution)/shard_map/ppermute | solution.py:34
  11.5 2.6 %collective-permute-start.1 = (bf16[2,2,128,128]{3,2,1,0:T(8,128)(2,1)S(1)}, bf16[2,2,128,128]{3,2,1,0:T(8,128)(2,1)S(1)}, u32[]{:S(2)}, u32[]{:S(2)}) collective-permute-start(bf16[2,2,128,128]{3,2,1,0:T(8,128)(2,1)S(1)} %get-tuple-element.405), channel_id=1, source_target_pairs={{0,8},{4,12},{8,0},{12,4},{1,9},{5,13},{9,1},{13,5},{2,10},{6,14},... | collective-permute-start | bytes 393224 | tf_op jit(solution)/shard_map/ppermute | solution.py:34
  14.1 1.3 collective-permute-start.2
  17.1 1.3 convolution_convert_fusion.1
  19.3 23.7 %all_gather.30 = bf16[2,512,256]{2,1,0:T(8,128)(2,1)} all-gather(bf16[2,128,256]{2,1,0:T(8,128)(2,1)S(1)} %copy-done.13), channel_id=1, replica_groups=mesh['groups'=2,'seq'=4,'head'=2,'sub'=2] {'seq'}, dimensions={1}, use_global_device_ids=true | all-gather | bytes 655360 | tf_op jit(solution)/shard_map/all_gather | solution.py:98
  43.8 13.6 %while.49 = (s32[]{:T(128)}, f32[2,1024]{1,0:T(2,128)S(1)}, f32[2,1024]{1,0:T(2,128)S(1)}, f32[2,1024,128]{2,1,0:T(8,128)S(1)}, bf16[2,512,256]{2,1,0:T(8,128)(2...) while((s32[]{:T(128)}, f32[2,1024]{1,0:T(2,128)S(1)}, ...), condition=%wide.region_7.8_spmd.clone, body=%wide.region_4.7_spmd.clone.sunk | while | flops 137505920 | bytes 6563051 | solution.py:128
  44.0 1.2 fusion.88
  45.5 1.6 %convolution_add_fusion.5 = f32[2,1024,128]{2,1,0:T(8,128)S(1)} fusion(f32[2,1024,128]{2,1,0:T(8,128)S(1)} %get-tuple-element.605, f32[2,1024,128]{1,2,0:T(8,128)S(1)} %get-tuple-element.560, f32[2,1024]{1,0:T(2,128)S(1)} %get-tuple-element.562, f32[2,1024]{1,0:T(2,128)S(1)} %fusion.89, pred[]{:T(512)S(6)} %compare.20, ...), kind=kOutput, calls=%fused_computation.15.clone.1 | convolution fusion | flops 68681728 | bytes 3358729 | tf_op jit(solution)/shard_map/while/body/eval_jaxpr/grk,gkd->grd/dot_general | solution.py:120
  47.4 1.2 fusion.88
  48.9 1.6 %convolution_add_fusion.5 = f32[2,1024,128]{2,1,0:T(8,128)S(1)} fusion(f32[2,1024,128]{2,1,0:T(8,128)S(1)} %get-tuple-element.605, f32[2,1024,128]{1,2,0:T(8,128)S(1)} %get-tuple-element.560, f32[2,1024]{1,0:T(2,128)S(1)} %get-tuple-element.562, f32[2,1024]{1,0:T(2,128)S(1)} %fusion.89, pred[]{:T(512)S(6)} %compare.20, ...), kind=kOutput, calls=%fused_computation.15.clone.1 | convolution fusion | flops 68681728 | bytes 3358729 | tf_op jit(solution)/shard_map/while/body/eval_jaxpr/grk,gkd->grd/dot_general | solution.py:120
  50.8 1.2 fusion.88
  52.3 1.6 %convolution_add_fusion.5 = f32[2,1024,128]{2,1,0:T(8,128)S(1)} fusion(f32[2,1024,128]{2,1,0:T(8,128)S(1)} %get-tuple-element.605, f32[2,1024,128]{1,2,0:T(8,128)S(1)} %get-tuple-element.560, f32[2,1024]{1,0:T(2,128)S(1)} %get-tuple-element.562, f32[2,1024]{1,0:T(2,128)S(1)} %fusion.89, pred[]{:T(512)S(6)} %compare.20, ...), kind=kOutput, calls=%fused_computation.15.clone.1 | convolution fusion | flops 68681728 | bytes 3358729 | tf_op jit(solution)/shard_map/while/body/eval_jaxpr/grk,gkd->grd/dot_general | solution.py:120
  54.2 1.2 fusion.88
  55.8 1.6 %convolution_add_fusion.5 = f32[2,1024,128]{2,1,0:T(8,128)S(1)} fusion(f32[2,1024,128]{2,1,0:T(8,128)S(1)} %get-tuple-element.605, f32[2,1024,128]{1,2,0:T(8,128)S(1)} %get-tuple-element.560, f32[2,1024]{1,0:T(2,128)S(1)} %get-tuple-element.562, f32[2,1024]{1,0:T(2,128)S(1)} %fusion.89, pred[]{:T(512)S(6)} %compare.20, ...), kind=kOutput, calls=%fused_computation.15.clone.1 | convolution fusion | flops 68681728 | bytes 3358729 | tf_op jit(solution)/shard_map/while/body/eval_jaxpr/grk,gkd->grd/dot_general | solution.py:120
  58.8 4.3 %all-to-all-start = ((bf16[2,8,128,128]{2,3,0,1:T(8,128)(2,1)}), bf16[2,8,128,128]{2,3,0,1:T(8,128)(2,1)S(1)}, u32[]{:S(2)}, u32[]{:S(2)}) async-start(bf16[2,8,128,128]{2,3,0,1:T(8,128)(2,1)} %copy.127), calls=%async_computation | async-start | bytes 1048576 | tf_op jit(solution)/shard_map/all_to_all | solution.py:168
  65.6 12.2 %all-reduce = bf16[64]{0:T(256)(128)(2,1)S(1)} all-reduce(bf16[64]{0:T(256)(128)(2,1)S(1)} %dynamic-update-slice), channel_id=2, replica_groups=mesh['groups'=2,'seq'=4,'head'=2,'sub'=2] {'seq'}, use_global_device_ids=true, to_apply=%add | all-reduce | flops 64 | bytes 256
  79.6 2.2 %fusion.51 = f32[16,128,128]{1,2,0:T(8,128)} fusion(f32[16,128,128]{2,1,0:T(8,128)S(1)} %bitcast_multiply_fusion.1, bf16[16,128,128]{2,1,0:T(8,128)(2,1)S(1)} %copy-done), kind=kOutput, calls=%fused_computation.115 | convolution fusion | flops 402653184 | bytes 2621440 | tf_op jit(solution)/shard_map/hts,hsp->htp/dot_general | solution.py:194
  83.4 3.3 %multiply_reduce_fusion.3 = (f32[16,128]{1,0:T(8,128)S(1)}, f32[16,128,128]{1,2,0:T(8,128)S(1)}) fusion(bf16[16,128,128]{1,2,0:T(8,128)(2,1)S(1)} %copy.121, f32[16]{0:T(128)S(1)} %copy-done.15, f32[16,128,128]{1,2,0:T(8,128)} %fusion.51, f32[16,128,64]{1,2,0:T(8,128)S(1)} %bitcast.115, f32[16,64,128]{2,1,0:T(8,128)S(1)} %get-tuple-element.293, ...), kind=kOutput, calls=%fused_computation.68 | convolution fusion | flops 203421696 | bytes 4210816 | tf_op jit(solution)/shard_map/htn,hnp->htp/dot_general | solution.py:204
  87.2 1.8 %multiply_reduce_fusion = (f32[16,128]{1,0:T(8,128)S(1)}, f32[16,128,128]{1,2,0:T(8,128)S(1)}) fusion(f32[16,128,128]{1,2,0:T(8,128)S(1)} %get-tuple-element.413, f32[16,128]{1,0:T(8,128)S(1)} %broadcast_multiply_fusion, f32[16,128]{1,0:T(8,128)S(1)} %fusion.40, f32[2,8,128,128]{2,3,1,0:T(8,128)} %copy-done.4, f32[16,128]{1,0:T(8,128)S(1)} %add_rsqrt_fusion, ...), kind=kLoop, calls=%fused_computation.63 | loop fusion | flops 2881536 | bytes 3702848 | tf_op jit(solution)/shard_map/reduce_sum | solution.py:220
  88.9 2.8 %convolution_convert_fusion = bf16[16,64,128]{2,1,0:T(8,128)(2,1)} fusion(f32[16,128,128]{1,2,0:T(8,128)S(1)} %get-tuple-element.397, f32[16,128,64]{1,2,0:T(8,128)S(1)} %bitcast.116, f32[16,128]{1,0:T(8,128)S(1)} %get-tuple-element.411), kind=kOutput, calls=%fused_computation.52 | convolution fusion | flops 201588736 | bytes 1843200 | tf_op jit(solution)/shard_map/htn,htp->hnp/dot_general | solution.py:221
  91.8 3.3 %fusion.28 = (f32[16,128]{1,0:T(8,128)S(1)}, f32[16,128,128]{1,2,0:T(8,128)}) fusion(bf16[16,128,128]{1,2,0:T(8,128)(2,1)S(1)} %copy.121, f32[16,128,128]{2,1,0:T(8,128)} %copy-done.1, f32[16,128,128]{1,2,0:T(8,128)S(1)} %get-tuple-element.397), kind=kOutput, calls=%fused_computation.55 | convolution fusion | flops 403437568 | bytes 3678208 | tf_op jit(solution)/shard_map/hts,htp->hsp/dot_general | solution.py:212
  95.5 12.4 %all-reduce.1 = bf16[64]{0:T(256)(128)(2,1)S(1)} all-reduce(bf16[64]{0:T(256)(128)(2,1)S(1)} %dynamic-update-slice.1), channel_id=5, replica_groups=mesh['groups'=2,'seq'=4,'head'=2,'sub'=2] {'seq'}, use_global_device_ids=true, to_apply=%add.1 | all-reduce | flops 64 | bytes 256
  108.0 2.1 %convolution_multiply_fusion.3 = f32[16,128,64]{1,2,0:T(8,128)S(1)} fusion(f32[16,128,128]{1,2,0:T(8,128)S(1)} %get-tuple-element.397, f32[16,128]{1,0:T(8,128)S(1)} %get-tuple-element.411, f32[16,64,128]{2,1,0:T(8,128)S(1)} %get-tuple-element.293, f32[16,64,128]{2,1,0:T(8,128)} %param.19, f32[16]{0:T(128)S(1)} %get-tuple-element.294), kind=kOutput, calls=%fused_computation.47 | convolution fusion | flops 201719808 | bytes 2629696 | tf_op jit(solution)/shard_map/hnp,htp->htn/dot_general | solution.py:217
  110.1 1.2 convolution_multiply_fusion.1
  112.4 2.9 %convolution_add_fusion.2 = f32[16,128,64]{1,2,0:T(8,128)} fusion(f32[16,128,64]{1,2,0:T(8,128)S(1)} %convolution_multiply_fusion.3, f32[16,128,128]{2,1,0:T(8,128)S(1)} %convolution_multiply_fusion.1, f32[16,128,64]{1,2,0:T(8,128)S(1)} %bitcast.119), kind=kOutput, calls=%fused_computation.48 | convolution fusion | flops 201457664 | bytes 2621440 | tf_op jit(solution)/shard_map/hts,hsn->htn/dot_general | solution.py:216
  115.3 6.2 %all-gather.9.cloned.1.call-done = bf16[64,64,128]{2,1,0:T(8,128)(2,1)} async-done(((bf16[16,64,128]{2,1,0:T(8,128)(2,1)}), bf16[64,64,128]{2,1,0:T(8,128)(2,1)}) %all-gather.9.cloned.1.call-update) | async-done | bytes 1048592 | tf_op jit(solution)/shard_map/all_gather | solution.py:72
  121.6 4.4 %while.48 = (s32[]{:T(128)}, f32[16,64,128]{2,1,0:T(8,128)S(1)}, f32[16]{0:T(128)S(1)}, s32[]{:T(128)}, bf16[4,16]{1,0:T(4,128)(2,1)S(1)}, /*index=5*/bf16[4,16,...) while((s32[]{:T(128)}, f32[16,64,128]{2,1,0:T(8,128)S(1)}, ...), condition=%wide.region_15.16_spmd, body=%wide.region_13.15_spmd.sunk | while | flops 786486 | bytes 1573487 | solution.py:89
  121.6 1.3 fusion.83
  123.0 1.3 fusion.83
  124.4 1.3 fusion.83
  127.3 2.8 %fusion.29 = (f32[16,128]{1,0:T(8,128)S(1)}, bf16[16,128,128]{1,2,0:T(8,128)(2,1)}) fusion(bf16[16,128,128]{1,2,0:T(8,128)(2,1)S(1)} %copy.121, f32[16,128,128]{1,2,0:T(8,128)S(1)} %get-tuple-element.397, f32[16]{0:T(128)S(1)} %copy-done.15, f32[16,128,128]{1,2,0:T(8,128)S(1)} %copy-done.8, f32[16,64,128]{2,1,0:T(8,128)S(1)} %get-tuple-element.297, ...), kind=kOutput, calls=%fused_computation.56 | convolution fusion | flops 203290624 | bytes 4210752 | tf_op jit(solution)/shard_map/hsn,hnp->hsp/dot_general | solution.py:234
  133.2 1.2 reduce_window_sum.22
  (129 shorter events, 20.2 us)
Async XLA Ops:
  7.2 74.9 %all-gather.7.cloned.1.call-start = ((), (), s32[]{:S(2)}) async-start(), calls=%async_computation.1 | async-start | bytes 1310720 | tf_op jit(solution)/shard_map/all_gather | solution.py:50
  7.3 8.2 %copy-start.14 = (f32[16,128]{1,0:T(8,128)S(1)}, f32[16,128]{1,0:T(8,128)}, u32[]{:S(2)}) copy-start(f32[16,128]{1,0:T(8,128)} %param.17) | copy-start | bytes 24580
  7.3 8.8 %copy-start.12 = (bf16[2,128,128]{2,1,0:T(8,128)(2,1)S(1)}, bf16[2,128,128]{2,1,0:T(8,128)(2,1)}, u32[]{:S(2)}) copy-start(bf16[2,128,128]{2,1,0:T(8,128)(2,1)} %param.16) | copy-start | bytes 196612
  8.5 8.7 %copy-start = (bf16[16,128,128]{2,1,0:T(8,128)(2,1)S(1)}, bf16[16,128,128]{2,1,0:T(8,128)(2,1)}, u32[]{:S(2)}) copy-start(bf16[16,128,128]{2,1,0:T(8,128)(2,1)} %param.15) | copy-start | bytes 1572868
  8.5 34.5 %collective-permute-start = (bf16[2,2,128,128]{3,2,1,0:T(8,128)(2,1)S(1)}, bf16[2,2,128,128]{3,2,1,0:T(8,128)(2,1)S(1)}, u32[]{:S(2)}, u32[]{:S(2)}) collective-permute-start(bf16[2,2,128,128]{3,2,1,0:T(8,128)(2,1)S(1)} %get-tuple-element.406), channel_id=1, source_target_pairs={{0,4},{4,8},{8,12},{12,0},{1,5},{5,9},{9,13},{13,1},{2,6},{6,10},{... | collective-permute-start | bytes 393224 | tf_op jit(solution)/shard_map/ppermute | solution.py:34
  11.5 31.4 %collective-permute-start.1 = (bf16[2,2,128,128]{3,2,1,0:T(8,128)(2,1)S(1)}, bf16[2,2,128,128]{3,2,1,0:T(8,128)(2,1)S(1)}, u32[]{:S(2)}, u32[]{:S(2)}) collective-permute-start(bf16[2,2,128,128]{3,2,1,0:T(8,128)(2,1)S(1)} %get-tuple-element.405), channel_id=1, source_target_pairs={{0,8},{4,12},{8,0},{12,4},{1,9},{5,13},{9,1},{13,5},{2,10},{6,14},... | collective-permute-start | bytes 393224 | tf_op jit(solution)/shard_map/ppermute | solution.py:34
  14.1 28.9 %collective-permute-start.2 = (bf16[2,2,128,128]{3,2,1,0:T(8,128)(2,1)S(1)}, bf16[2,2,128,128]{3,2,1,0:T(8,128)(2,1)S(1)}, u32[]{:S(2)}, u32[]{:S(2)}) collective-permute-start(bf16[2,2,128,128]{3,2,1,0:T(8,128)(2,1)S(1)} %get-tuple-element.407), channel_id=1, source_target_pairs={{0,12},{4,0},{8,4},{12,8},{1,13},{5,1},{9,5},{13,9},{2,14},{6,2},{... | collective-permute-start | bytes 393224 | tf_op jit(solution)/shard_map/ppermute | solution.py:34
  16.3 0.8 copy-start.5
  18.4 0.9 copy-start.13
  58.8 23.1 %all-to-all-start = ((bf16[2,8,128,128]{2,3,0,1:T(8,128)(2,1)}), bf16[2,8,128,128]{2,3,0,1:T(8,128)(2,1)S(1)}, u32[]{:S(2)}, u32[]{:S(2)}) async-start(bf16[2,8,128,128]{2,3,0,1:T(8,128)(2,1)} %copy.127), calls=%async_computation | async-start | bytes 1048576 | tf_op jit(solution)/shard_map/all_to_all | solution.py:168
  63.0 58.5 %all-gather.9.cloned.1.call-start = ((), (), s32[]{:S(2)}) async-start(), calls=%async_computation.2 | async-start | bytes 1310720 | tf_op jit(solution)/shard_map/all_gather | solution.py:72
  63.3 0.7 copy-start.16
  78.6 1.0 copy-start.1
  81.9 4.8 %copy-start.4 = (f32[2,8,128,128]{2,3,1,0:T(8,128)}, f32[2,8,128,128]{2,3,1,0:T(8,128)S(1)}, u32[]{:S(2)}) copy-start(f32[2,8,128,128]{2,3,1,0:T(8,128)S(1)} %copy.128) | copy-start | bytes 3145732
  82.4 1.0 copy-start.11
  82.4 1.0 copy-start.15
  110.1 2.3 %copy-start.6 = (f32[2,8,128,64]{2,3,1,0:T(8,128)S(1)}, f32[2,8,128,64]{2,3,1,0:T(8,128)}, u32[]{:S(2)}) copy-start(f32[2,8,128,64]{2,3,1,0:T(8,128)} %copy-done.5) | copy-start | bytes 1572868
  111.3 1.0 copy-start.2
  126.0 1.2 copy-start.8
  126.0 1.3 copy-start.7
  127.3 2.8 %copy-start.3 = (f32[16,128,128]{2,1,0:T(8,128)S(1)}, f32[16,128,128]{2,1,0:T(8,128)}, u32[]{:S(2)}) copy-start(f32[16,128,128]{2,1,0:T(8,128)} %copy-done.2) | copy-start | bytes 3145732
  130.1 1.0 copy-start.9
  131.2 1.0 copy-start.10
Sparse Core Ops, SparseCore 0:
  18.5 32.5 all-gather.6
  91.9 29.5 all-gather.8
